TPU v7x, 128 devices: a whole 4x4x4 slice. The times are simulated.
128 devices in a mesh: tok: 16 (over y, x), head: 8 (over z, core).
Axes of the slice: x: 4, y: 4, z: 4, core: 2. Of those that a mesh axis runs over, the one named last changes fastest.
Arguments:
- tokens: bfloat16 [8192, 8192], P('tok', 'head'), may hold values from -60 to 60
- gain: bfloat16 [8192], P('head'), may hold values from 0.5 to 2
- w_query: bfloat16 [8192, 8, 512], P(('head', 'tok')), may hold values from -0.125 to 0.125
- w_key: bfloat16 [8192, 8, 128], P(('head', 'tok')), may hold values from -0.0625 to 0.0625
- w_value: bfloat16 [8192, 8, 128], P(('head', 'tok')), may hold values from -0.5 to 0.5
- group_ids: int32 [8192, 1], P('tok'), may hold values from 0 to 15; in each aligned block of 512 rows (0 to 511, 512 to 1023, ...) at most 64 rows name the same one
- key_pages: bfloat16 [1024, 128, 8, 128], P('tok', None, 'head'), may hold values from -42 to 42
- value_pages: bfloat16 [1024, 128, 8, 128], P('tok', None, 'head'), may hold values from -48 to 48
- page_table: int32 [16, 32], P('tok'), may hold values from 0 to 1023, as said below
Outputs:
- attention: bfloat16 [8192, 4096], P('tok', 'head')
Inputs may be any that keep to these rules, and one draw needn't show every extreme that they name: `group_ids`: among the 512 tokens of one index of tok (aligned blocks of rows), no group appears more than 64 times, a bound that some block reaches. `page_table`: row g lists 32 different pages, all in g * 64 to (g + 1) * 64 - 1, among them the first and the last page of that range.
All inputs are finite; a program needn't handle non-finite values.
Results may differ from a plain program's by a relative error of at most 0.0085.
The roundings to bfloat16 on the way count: a program that leaves them out, or rounds other values in their place, can miss the bound.
Values may be sent and summed in bfloat16 or wider, within the bound.
No kernel may reach another device: no remote copies, remote signals or barrier semaphores. Data moves between devices by JAX's collectives and lax.ppermute only.
A program may use at most 128 MiB of HBM per device.

v0:
```python
import math
import jax
import jax.numpy as jnp
from jax import lax
from jax.sharding import PartitionSpec as P

EPS = 1e-05
THETA = 10000.0


def rotate(values, positions):
    halfway = values.shape[-1] // 2
    frequency = jnp.exp(
        -math.log(THETA) * 2.0 * jnp.arange(halfway, dtype=jnp.float32) / values.shape[-1]
    )
    angles = positions.astype(jnp.float32)[:, None] * frequency[None, :]
    cosine = jnp.cos(angles)[:, None, :]
    sine_part = jnp.sin(angles)[:, None, :]
    leading = values[..., :halfway].astype(jnp.float32)
    trailing = values[..., halfway:].astype(jnp.float32)
    return jnp.concatenate(
        [leading * cosine - trailing * sine_part, trailing * cosine + leading * sine_part], axis=-1
    ).astype(jnp.bfloat16)


def attend(
    queries, query_rank, prefix_keys, prefix_values, new_keys, new_values, key_rank, key_live
):
    scaling = 1.0 / math.sqrt(queries.shape[-1])
    before = (
        jnp.einsum("bhd,pd->bhp", queries, prefix_keys, preferred_element_type=jnp.float32)
        * scaling
    )
    inside = (
        jnp.einsum("bhd,sd->bhs", queries, new_keys, preferred_element_type=jnp.float32) * scaling
    )
    allowed = key_live[None, :] & (key_rank[None, :] <= query_rank[:, None])
    inside = jnp.where(allowed[:, None, :], inside, -jnp.inf)
    highest = jnp.maximum(jnp.max(before, axis=-1), jnp.max(inside, axis=-1))
    expo_before = jnp.exp(before - highest[..., None])
    expo_inside = jnp.exp(inside - highest[..., None])
    totals = jnp.sum(expo_before, axis=-1) + jnp.sum(expo_inside, axis=-1)
    mixed = jnp.einsum(
        "bhp,pd->bhd",
        expo_before.astype(jnp.bfloat16),
        prefix_values,
        preferred_element_type=jnp.float32,
    )
    mixed = mixed + jnp.einsum(
        "bhs,sd->bhd",
        expo_inside.astype(jnp.bfloat16),
        new_values,
        preferred_element_type=jnp.float32,
    )
    return (mixed / totals[..., None]).astype(jnp.bfloat16)


def row_norm(tokens, gain, full_width):
    values_wide = tokens.astype(jnp.float32)
    squares = lax.psum(jnp.sum(values_wide * values_wide, axis=1), "head")
    factor = lax.rsqrt(squares / full_width + EPS)
    return (values_wide * factor[:, None] * gain.astype(jnp.float32)[None, :]).astype(jnp.bfloat16)


def body(tokens, gain, w_query, w_key, w_value, group_ids, key_pages, value_pages, page_table):
    row_count = tokens.shape[0]
    n_tok = lax.axis_size("tok")
    n_head = lax.axis_size("head")
    head_size = key_pages.shape[-1]
    query_width = w_query.shape[2]
    group_heads = query_width // head_size
    full_width = tokens.shape[1] * n_head
    capacity = 2 * row_count // n_tok
    normed = row_norm(tokens, gain, full_width)
    weights_local = jnp.concatenate([w_query, w_key, w_value], axis=2)
    gathered = lax.all_gather(weights_local, "tok", axis=0, tiled=True)
    group_count = row_count * lax.axis_size("head") // row_count
    joined = jnp.einsum("rd,dnc->nrc", normed, gathered, preferred_element_type=jnp.float32)
    projected = lax.psum_scatter(
        joined.reshape(group_count * row_count, joined.shape[2]),
        "head",
        scatter_dimension=0,
        tiled=True,
    )
    projected_low = projected.astype(jnp.bfloat16)
    width_all = projected_low.shape[1]
    group_of = group_ids[:, 0]
    member = (group_of[:, None] == jnp.arange(n_tok, dtype=jnp.int32)[None, :]).astype(jnp.int32)
    local_rank = jnp.sum((jnp.cumsum(member, axis=0) - member) * member, axis=1)
    slot_index = group_of * capacity + local_rank
    counts_local = jnp.sum(member, axis=0).astype(jnp.bfloat16)
    outgoing = (
        jnp.zeros((n_tok * capacity, width_all), jnp.bfloat16).at[slot_index].set(projected_low)
    )
    count_rows = jnp.broadcast_to(counts_local[:, None, None], (n_tok, 16, width_all))
    outgoing = jnp.concatenate([outgoing.reshape(n_tok, capacity, width_all), count_rows], axis=1)
    arrived_all = lax.all_to_all(outgoing, "tok", split_axis=0, concat_axis=0, tiled=True)
    block_counts = arrived_all[:, capacity, 0].astype(jnp.int32)
    arrived = arrived_all[:, :capacity, :]
    slot_total = n_tok * capacity
    arrived = arrived.reshape(slot_total, width_all)
    live_count = (
        (jnp.arange(capacity, dtype=jnp.int32)[None, :] < block_counts[:, None])
        .astype(jnp.int32)
        .reshape(slot_total)
    )
    key_live = live_count > 0
    slot_rank = jnp.cumsum(live_count) - live_count
    prefix_length = page_table.shape[1] * key_pages.shape[1]
    positions = prefix_length + slot_rank
    rotated_queries = rotate(
        arrived[:, :query_width].reshape(slot_total, group_heads, head_size), positions
    )
    rotated_keys = rotate(
        arrived[:, query_width : query_width + head_size].reshape(slot_total, 1, head_size),
        positions,
    )[:, 0, :]
    slot_values = arrived[:, query_width + head_size :]
    local_pages = page_table[0] - lax.axis_index("tok") * key_pages.shape[0]
    prefix_keys = jnp.take(key_pages[:, :, 0, :], local_pages, axis=0).reshape(
        prefix_length, head_size
    )
    prefix_values = jnp.take(value_pages[:, :, 0, :], local_pages, axis=0).reshape(
        prefix_length, head_size
    )
    block_size = min(128, slot_total)

    def one_block(blocked):
        return attend(
            blocked[0],
            blocked[1],
            prefix_keys,
            prefix_values,
            rotated_keys,
            slot_values,
            slot_rank,
            key_live,
        )

    attended = lax.map(
        one_block,
        (
            rotated_queries.reshape(slot_total // block_size, block_size, group_heads, head_size),
            slot_rank.reshape(slot_total // block_size, block_size),
        ),
    )
    returned = lax.all_to_all(
        attended.reshape(n_tok, capacity, query_width),
        "tok",
        split_axis=0,
        concat_axis=0,
        tiled=True,
    )
    return returned.reshape(n_tok * capacity, query_width)[slot_index]


def solution(mesh):
    placed = (
        P("tok", "head"),
        P("head"),
        P(("head", "tok"), None, None),
        P(("head", "tok"), None, None),
        P(("head", "tok"), None, None),
        P("tok", None),
        P("tok", None, "head", None),
        P("tok", None, "head", None),
        P("tok", None),
    )
    return jax.shard_map(
        body, mesh=mesh, in_specs=placed, out_specs=P("tok", "head"), check_vma=False
    )
```

profile of v0, /device:TPU:32, one launch (start us, length us, event | category | flops | bytes accessed | tf_op | source)
XLA Modules:
  0.0 343.7 jit_solution(11092186876331091009)
XLA Ops:
  6.5 1.3 copy.23
  7.9 0.9 copy.24
  8.8 0.9 copy.25
  9.8 1.0 pad_maximum_fusion.2
  11.1 12.5 %psum.7 = f32[512]{0:T(512)S(1)} all-reduce(f32[512]{0:T(512)S(1)} %fusion.33), channel_id=1, replica_groups=mesh['tok'=16,'head'=8] {'head'}, use_global_device_ids=true, to_apply=%region_4.5 | all-reduce | flops 512 | bytes 4096 | tf_op jit(solution)/shard_map/psum | solution.py:60
  23.6 78.9 %all-gather.2.cloned.1.call-done = bf16[1024,8,768]{2,0,1:T(8,128)(2,1)} async-done(((bf16[64,8,768]{2,0,1:T(8,128)(2,1)}), bf16[1024,8,768]{2,0,1:T(8,128)(2,1)}) %all-gather.2.cloned.1.call-update) | async-done | bytes 12582928 | tf_op jit(solution)/shard_map/all_gather | solution.py:76
  102.5 14.4 %fusion.41 = f32[8,768,512]{1,2,0:T(8,128)} fusion(bf16[1024,8,768]{2,0,1:T(8,128)(2,1)} %all-gather.2.cloned.1.call-done, bf16[512,1024]{1,0:T(8,128)(2,1)S(1)} %copy-done.3, f32[1024]{0:T(1024)S(1)} %convert_element_type.95, f32[512]{0:T(512)S(1)} %add_rsqrt_fusion), kind=kOutput, calls=%fused_computation.59 | convolution fusion | flops 6444548096 | bytes 26220544 | tf_op jit(solution)/shard_map/rd,dnc->nrc/dot_general | solution.py:78
  117.6 1.1 reduce-window.15
  119.2 67.6 %reduce-scatter.2.cloned.1.call-done = f32[512,768]{1,0:T(8,128)} async-done(((f32[4096,768]{1,0:T(8,128)}), f32[512,768]{1,0:T(8,128)}) %reduce-scatter.2.cloned.1.call-update) | async-done | bytes 1572880 | tf_op jit(solution)/shard_map/reduce_scatter | solution.py:79
  186.7 4.6 %scatter_custom_fusion = bf16[1024,768]{1,0:T(8,128)(2,1)} fusion(s32[512]{0:T(512)S(1)} %bitcast.115, f32[512,768]{1,0:T(8,128)} %reduce-scatter.2.cloned.1.call-done, bf16[]{:T(256)} %constant.32.clone.1), kind=kCustom, calls=%fused_computation.66 | custom fusion | flops 393216 | bytes 3145730 | tf_op jit(solution)/shard_map/scatter | solution.py:93
  191.5 2.8 pad_maximum_fusion
  194.3 7.2 %all-to-all-start = ((bf16[16,80,768]{2,1,0:T(8,128)(2,1)}), bf16[16,80,768]{2,1,0:T(8,128)(2,1)}, u32[]{:S(2)}, u32[]{:S(2)}) async-start(bf16[16,80,768]{2,1,0:T(8,128)(2,1)} %pad_maximum_fusion), calls=%async_computation.1 | async-start | bytes 3932160 | tf_op jit(solution)/shard_map/all_to_all | solution.py:97
  201.7 0.7 gather_fusion.1
  202.4 3.3 gather_fusion.2
  205.7 1.5 broadcast_select_fusion
  207.2 27.9 %all-to-all-done = bf16[16,80,768]{2,1,0:T(8,128)(2,1)} async-done(((bf16[16,80,768]{2,1,0:T(8,128)(2,1)}), bf16[16,80,768]{2,1,0:T(8,128)(2,1)}, u32[]{:S(2)}, u32[]{:S(2)}) %all-to-all-start) | async-done | bytes 1966112 | tf_op jit(solution)/shard_map/all_to_all | solution.py:97
  235.1 1.1 fusion.61
  236.4 1.6 slice.60
  237.9 0.8 fusion.63
  239.6 1.8 multiply_cosine_fusion.1
  241.4 3.1 fusion.57
  244.6 1.3 copy.30
  245.9 1.6 fusion.37
  247.7 1.1 pad_maximum_fusion.1
  248.8 1.7 copy.28
  250.6 1.2 pad_maximum_fusion.3
  251.7 58.3 %while.11 = (s32[]{:T(128)}, bf16[8,128,4,128]{3,2,1,0:T(4,128)(2,1)}, bf16[8,128,4,128]{3,1,2,0:T(8,128)(2,1)S(1)}, bf16[4096,128]{1,0:T(8,128)(2,1)S(1)}, s32[...) while((s32[]{:T(128)}, ...), condition=%wide.region_15.17_spmd.clone, body=%wide.region_10.16_spmd.clone.sunk | while | flops 1365182464 | bytes 36886740 | solution.py:140
  252.6 1.3 multiply_reduce_fusion.2
  254.6 1.5 fusion.84
  256.1 1.5 fusion.83
  258.3 0.7 copy_dynamic-update-slice_fusion.2
  259.9 1.3 multiply_reduce_fusion.2
  261.9 1.5 fusion.84
  263.4 1.5 fusion.83
  264.9 0.7 fusion.86
  265.6 0.8 copy_dynamic-update-slice_fusion.2
  267.2 1.3 multiply_reduce_fusion.2
  269.2 1.5 fusion.84
  270.7 1.5 fusion.83
  272.9 0.8 copy_dynamic-update-slice_fusion.2
  274.5 1.3 multiply_reduce_fusion.2
  276.4 1.5 fusion.84
  278.0 1.5 fusion.83
  280.1 0.7 copy_dynamic-update-slice_fusion.2
  281.8 1.3 multiply_reduce_fusion.2
  283.7 1.5 fusion.84
  285.2 1.5 fusion.83
  287.4 0.8 copy_dynamic-update-slice_fusion.2
  289.1 1.3 multiply_reduce_fusion.2
  291.0 1.5 fusion.84
  292.5 1.5 fusion.83
  294.7 0.8 copy_dynamic-update-slice_fusion.2
  296.4 1.3 multiply_reduce_fusion.2
  298.3 1.5 fusion.84
  299.8 1.5 fusion.83
  302.0 0.8 copy_dynamic-update-slice_fusion.2
  303.6 1.3 multiply_reduce_fusion.2
  305.6 1.5 fusion.84
  307.1 1.5 fusion.83
  309.3 0.8 copy_dynamic-update-slice_fusion.2
  310.0 2.3 reshape.292
  312.3 3.7 %all-to-all-start.1 = ((bf16[16,64,512]{2,1,0:T(8,128)(2,1)}), bf16[16,64,512]{2,1,0:T(8,128)(2,1)S(1)}, u32[]{:S(2)}, u32[]{:S(2)}) async-start(bf16[16,64,512]{2,1,0:T(8,128)(2,1)} %reshape.292), calls=%async_computation.2 | async-start | bytes 2097152 | tf_op jit(solution)/shard_map/all_to_all | solution.py:147
  316.0 18.2 %all-to-all-done.1 = bf16[16,64,512]{2,1,0:T(8,128)(2,1)S(1)} async-done(((bf16[16,64,512]{2,1,0:T(8,128)(2,1)}), bf16[16,64,512]{2,1,0:T(8,128)(2,1)S(1)}, u32[]{:S(2)}, u32[]{:S(2)}) %all-to-all-start.1) | async-done | bytes 1048608 | tf_op jit(solution)/shard_map/all_to_all | solution.py:147
  334.2 2.6 gather_fusion
  (146 shorter events, 19.7 us)
Async XLA Ops:
  6.5 195.1 %copy-start = (bf16[64,128,1,128]{3,1,2,0:T(8,128)(2,1)S(1)}, bf16[64,128,1,128]{3,1,2,0:T(8,128)(2,1)}, u32[]{:S(2)}) copy-start(bf16[64,128,1,128]{3,1,2,0:T(8,128)(2,1)} %param.19) | copy-start | bytes 6291460
  6.5 4.2 %copy-start.6 = (bf16[1024]{0:T(1024)(128)(2,1)S(1)}, bf16[1024]{0:T(1024)(128)(2,1)}, u32[]{:S(2)}) copy-start(bf16[1024]{0:T(1024)(128)(2,1)} %param.14) | copy-start | bytes 6148
  6.5 4.3 %copy-start.3 = (bf16[512,1024]{1,0:T(8,128)(2,1)S(1)}, bf16[512,1024]{1,0:T(8,128)(2,1)}, u32[]{:S(2)}) copy-start(bf16[512,1024]{1,0:T(8,128)(2,1)} %param.13) | copy-start | bytes 3145732
  6.5 96.0 %all-gather.2.cloned.1.call-start = ((), (), s32[]{:S(2)}) async-start(), calls=%async_computation.3 | async-start | bytes 13369344 | tf_op jit(solution)/shard_map/all_gather | solution.py:76
  10.7 176.0 %reduce-scatter.2.cloned.1.call-start = ((), (), s32[]{:S(2)}) async-start(), calls=%async_computation.4 | async-start | bytes 14155776 | tf_op jit(solution)/shard_map/reduce_scatter | solution.py:79
  116.9 0.7 copy-start.5
  194.3 7.3 %copy-start.7 = (s32[1,32]{1,0:T(1,128)S(1)}, s32[1,32]{1,0:T(1,128)}, u32[]{:S(2)}) copy-start(s32[1,32]{1,0:T(1,128)} %param.21) | copy-start | bytes 388
  194.3 40.8 %all-to-all-start = ((bf16[16,80,768]{2,1,0:T(8,128)(2,1)}), bf16[16,80,768]{2,1,0:T(8,128)(2,1)}, u32[]{:S(2)}, u32[]{:S(2)}) async-start(bf16[16,80,768]{2,1,0:T(8,128)(2,1)} %pad_maximum_fusion), calls=%async_computation.1 | async-start | bytes 3932160 | tf_op jit(solution)/shard_map/all_to_all | solution.py:97
  244.6 1.3 copy-start.2
  256.1 1.5 copy-start.4
  263.4 1.5 copy-start.4
  270.7 1.5 copy-start.4
  277.9 1.5 copy-start.4
  285.2 1.5 copy-start.4
  292.5 1.5 copy-start.4
  299.8 1.5 copy-start.4
  307.1 1.5 copy-start.4
  312.3 21.9 %all-to-all-start.1 = ((bf16[16,64,512]{2,1,0:T(8,128)(2,1)}), bf16[16,64,512]{2,1,0:T(8,128)(2,1)S(1)}, u32[]{:S(2)}, u32[]{:S(2)}) async-start(bf16[16,64,512]{2,1,0:T(8,128)(2,1)} %reshape.292), calls=%async_computation.2 | async-start | bytes 2097152 | tf_op jit(solution)/shard_map/all_to_all | solution.py:147
  334.2 2.6 copy-start.1
Sparse Core Ops, SparseCore 0:
  10.9 91.6 all-gather.1
  117.1 69.6 reduce-scatter.1
where the time goes:
time: 344 us
  waiting for transfers between devices  193 us (56%)
  matrix products  46.8 us (14%)
  other arithmetic  40.8 us (12%)
  local copies, waits for them, and re-layouts  26 us (8%)
  between operations  13.6 us (4%)
  blocking collectives  12.5 us (4%)
  starting transfers between devices  10.9 us (3%)
    all_gather x1, waiting for transfers between devices, body(): gathered = lax.all_gather(weights_local, 'tok', axis=0, tiled=True)  78.9 us
    reduce_scatter x1, waiting for transfers between devices, body(): lax.psum_scatter(joined.reshape(group_count * row_count, joined.shape[2])...  67.6 us
    all_to_all x1, waiting for transfers between devices, body(): lax.all_to_all(outgoing, 'tok', split_axis=0, concat_axis=0, tiled=True)  27.9 us
    all_to_all x1, waiting for transfers between devices, body(): lax.all_to_all(attended.reshape(n_tok, capacity, query_width), 'tok', spl...  18.2 us
    reduce_sum x16, other arithmetic, attend(): totals = jnp.sum(expo_before, axis=-1) + jnp.sum(expo_inside, axis=-1)  16.8 us
    dot_general x1, matrix products, body(): jnp.einsum('rd,dnc->nrc', normed, gathered, preferred_element_type=jnp.fl...  14.4 us
    psum x1, blocking collectives, row_norm(): squares = lax.psum(jnp.sum(values_wide * values_wide, axis=1), 'head')  12.5 us
    dot_general x8, matrix products, attend(): jnp.einsum('bhp,pd->bhd', expo_before.astype(jnp.bfloat16), prefix_values...  11.8 us
  transfers between devices with their start and end apart: 4, of which 4 were waited for; matrix products, arithmetic and copies ran while one was open for 2% of the time, Pallas kernels for 0%

commit v1 on v0

--- a/solution.py
+++ b/solution.py
@@ -3,6 +3,7 @@
 import jax.numpy as jnp
 from jax import lax
 from jax.sharding import PartitionSpec as P
+from jax.lax import all_to_all, axis_size
 
 EPS = 1e-05
 THETA = 10000.0
@@ -73,7 +74,10 @@
     capacity = 2 * row_count // n_tok
     normed = row_norm(tokens, gain, full_width)
     weights_local = jnp.concatenate([w_query, w_key, w_value], axis=2)
-    gathered = lax.all_gather(weights_local, "tok", axis=0, tiled=True)
+    part_next = tuple((weights_local for _ in range(axis_size("tok"))))
+    inter = jnp.stack(part_next)
+    reached = all_to_all(inter, concat_axis=0, axis_name="tok", split_axis=0)
+    gathered = jnp.concatenate(reached, axis=0)
     group_count = row_count * lax.axis_size("head") // row_count
     joined = jnp.einsum("rd,dnc->nrc", normed, gathered, preferred_element_type=jnp.float32)
     projected = lax.psum_scatter(

time: 344 us -> 451 us (1.31)
  waiting for transfers between devices: 193 us -> 287 us
  local copies, waits for them, and re-layouts: 26 us -> 35.5 us
  starting transfers between devices: 10.9 us -> 18.1 us
  matrix products: 46.8 us -> 41.8 us
    all_to_all x0 -> x1, waiting for transfers between devices: none -> 174 us  [body(): reached = all_to_all(inter, concat_axis=0, axis_name='tok', split_axis=0)]
    all_gather x1 -> x0, waiting for transfers between devices: 78.9 us -> none  [body(): gathered = lax.all_gather(weights_local, 'tok', axis=0, tiled=True)]
    all_to_all x0 -> x1, starting transfers between devices: none -> 7.21 us  [body(): reached = all_to_all(inter, concat_axis=0, axis_name='tok', split_axis=0)]
    all_to_all x0 -> x1, local copies, waits for them, and re-layouts: none -> 6.52 us  [body(): reached = all_to_all(inter, concat_axis=0, axis_name='tok', split_axis=0)]
    another operation x3 -> x4, local copies, waits for them, and re-layouts: 0.2 us -> 6.24 us  [the longest x1 6.05 us: body(): inter = jnp.stack(part_next)]
    dot_general x1, matrix products: 14.4 us -> 9.34 us  [body(): jnp.einsum('rd,dnc->nrc', normed, gathered, preferred_element_type=jnp.fl...]
where the time goes in v1:
time: 451 us
  waiting for transfers between devices  287 us (64%)
  matrix products  41.8 us (9%)
  other arithmetic  41.2 us (9%)
  local copies, waits for them, and re-layouts  35.5 us (8%)
  starting transfers between devices  18.1 us (4%)
  between operations  13.6 us (3%)
  blocking collectives  12.6 us (3%)
    all_to_all x1, waiting for transfers between devices, body(): reached = all_to_all(inter, concat_axis=0, axis_name='tok', split_axis=0)  174 us
    reduce_scatter x1, waiting for transfers between devices, body(): lax.psum_scatter(joined.reshape(group_count * row_count, joined.shape[2])...  67.3 us
    all_to_all x1, waiting for transfers between devices, body(): lax.all_to_all(outgoing, 'tok', split_axis=0, concat_axis=0, tiled=True)  27.9 us
    all_to_all x1, waiting for transfers between devices, body(): lax.all_to_all(attended.reshape(n_tok, capacity, query_width), 'tok', spl...  18.2 us
    reduce_sum x16, other arithmetic, attend(): totals = jnp.sum(expo_before, axis=-1) + jnp.sum(expo_inside, axis=-1)  16.8 us
    psum x1, blocking collectives, row_norm(): squares = lax.psum(jnp.sum(values_wide * values_wide, axis=1), 'head')  12.6 us
    dot_general x8, matrix products, attend(): jnp.einsum('bhp,pd->bhd', expo_before.astype(jnp.bfloat16), prefix_values...  11.8 us
    dot_general x8, matrix products, attend(): jnp.einsum('bhd,pd->bhp', queries, prefix_keys, preferred_element_type=jn...  10.7 us
  transfers between devices with their start and end apart: 4, of which 4 were waited for; matrix products, arithmetic and copies ran while one was open for 2% of the time, Pallas kernels for 0%

profile of v1, /device:TPU:32, one launch (start us, length us, event | category | flops | bytes accessed | tf_op | source)
XLA Modules:
  0.0 450.8 jit_solution(7649650904428789595)
XLA Ops:
  6.5 1.4 pad_maximum_fusion.2
  8.1 6.0 %stack.2 = bf16[16,64,8,768]{3,1,2,0:T(8,128)(2,1)} broadcast(bf16[64,8,768]{2,0,1:T(8,128)(2,1)S(1)} %copy.25), dimensions={1,2,3} | broadcast | bytes 13369344 | tf_op jit(solution)/shard_map/stack | solution.py:78
  14.1 7.2 %all-to-all-start = ((bf16[16,64,8,768]{3,1,2,0:T(8,128)(2,1)}), bf16[16,64,8,768]{3,1,2,0:T(8,128)(2,1)}, u32[]{:S(2)}, u32[]{:S(2)}) async-start(bf16[16,64,8,768]{3,1,2,0:T(8,128)(2,1)} %stack.2), calls=%async_computation | async-start | bytes 25165824 | tf_op jit(solution)/shard_map/all_to_all | solution.py:79
  21.7 12.6 %psum.7 = f32[512]{0:T(512)S(1)} all-reduce(f32[512]{0:T(512)S(1)} %fusion.33), channel_id=1, replica_groups=mesh['tok'=16,'head'=8] {'head'}, use_global_device_ids=true, to_apply=%region_4.5 | all-reduce | flops 512 | bytes 4096 | tf_op jit(solution)/shard_map/psum | solution.py:61
  34.3 174.0 %all-to-all-done = bf16[16,64,8,768]{3,1,2,0:T(8,128)(2,1)} async-done(((bf16[16,64,8,768]{3,1,2,0:T(8,128)(2,1)}), bf16[16,64,8,768]{3,1,2,0:T(8,128)(2,1)}, u32[]{:S(2)}, u32[]{:S(2)}) %all-to-all-start) | async-done | bytes 12582944 | tf_op jit(solution)/shard_map/all_to_all | solution.py:79
  208.4 6.5 %copy.26 = bf16[16,64,8,768]{3,1,0,2:T(8,128)(2,1)S(1)} copy(bf16[16,64,8,768]{3,1,2,0:T(8,128)(2,1)} %all-to-all-done) | data formatting | bytes 25165824 | tf_op jit(solution)/shard_map/all_to_all | solution.py:79
  214.9 9.3 %fusion.41 = f32[8,768,512]{1,2,0:T(8,128)} fusion(bf16[1024,8,768]{2,0,1:T(8,128)(2,1)S(1)} %bitcast.105, bf16[512,1024]{1,0:T(8,128)(2,1)S(1)} %copy-done.3, f32[1024]{0:T(1024)S(1)} %convert_element_type.95, f32[512]{0:T(512)S(1)} %add_rsqrt_fusion), kind=kOutput, calls=%fused_computation.59 | convolution fusion | flops 6444548096 | bytes 26220544 | tf_op jit(solution)/shard_map/rd,dnc->nrc/dot_general | solution.py:82
  224.9 1.1 reduce-window.15
  226.5 67.3 %reduce-scatter.2.cloned.1.call-done = f32[512,768]{1,0:T(8,128)} async-done(((f32[4096,768]{1,0:T(8,128)}), f32[512,768]{1,0:T(8,128)}) %reduce-scatter.2.cloned.1.call-update) | async-done | bytes 1572880 | tf_op jit(solution)/shard_map/reduce_scatter | solution.py:83
  293.8 4.6 %scatter_custom_fusion = bf16[1024,768]{1,0:T(8,128)(2,1)} fusion(s32[512]{0:T(512)S(1)} %bitcast.117, f32[512,768]{1,0:T(8,128)} %reduce-scatter.2.cloned.1.call-done, bf16[]{:T(256)} %constant.32.clone.1), kind=kCustom, calls=%fused_computation.66 | custom fusion | flops 393216 | bytes 3145730 | tf_op jit(solution)/shard_map/scatter | solution.py:97
  298.6 2.8 pad_maximum_fusion
  301.4 7.2 %all-to-all-start.1 = ((bf16[16,80,768]{2,1,0:T(8,128)(2,1)}), bf16[16,80,768]{2,1,0:T(8,128)(2,1)}, u32[]{:S(2)}, u32[]{:S(2)}) async-start(bf16[16,80,768]{2,1,0:T(8,128)(2,1)} %pad_maximum_fusion), calls=%async_computation.2 | async-start | bytes 3932160 | tf_op jit(solution)/shard_map/all_to_all | solution.py:101
  308.7 0.7 gather_fusion.1
  309.5 3.3 gather_fusion.2
  312.8 1.5 broadcast_select_fusion
  314.2 27.9 %all-to-all-done.1 = bf16[16,80,768]{2,1,0:T(8,128)(2,1)} async-done(((bf16[16,80,768]{2,1,0:T(8,128)(2,1)}), bf16[16,80,768]{2,1,0:T(8,128)(2,1)}, u32[]{:S(2)}, u32[]{:S(2)}) %all-to-all-start.1) | async-done | bytes 1966112 | tf_op jit(solution)/shard_map/all_to_all | solution.py:101
  342.1 1.1 fusion.61
  343.4 1.6 slice.60
  345.0 0.8 fusion.63
  346.7 1.8 multiply_cosine_fusion.1
  348.5 3.1 fusion.57
  351.6 1.3 copy.31
  353.0 1.6 fusion.37
  354.8 1.1 pad_maximum_fusion.1
  355.9 1.7 copy.29
  357.6 1.2 pad_maximum_fusion.3
  358.8 58.3 %while.11 = (s32[]{:T(128)}, bf16[8,128,4,128]{3,2,1,0:T(4,128)(2,1)}, bf16[8,128,4,128]{3,1,2,0:T(8,128)(2,1)S(1)}, bf16[4096,128]{1,0:T(8,128)(2,1)S(1)}, s32[...) while((s32[]{:T(128)}, ...), condition=%wide.region_15.17_spmd.clone, body=%wide.region_10.16_spmd.clone.sunk | while | flops 1365182464 | bytes 36886740 | solution.py:144
  359.7 1.3 multiply_reduce_fusion.2
  361.6 1.5 fusion.84
  363.2 1.5 fusion.83
  364.7 0.7 fusion.86
  365.3 0.7 copy_dynamic-update-slice_fusion.2
  367.0 1.3 multiply_reduce_fusion.2
  368.9 1.5 fusion.84
  370.4 1.5 fusion.83
  372.6 0.8 copy_dynamic-update-slice_fusion.2
  374.3 1.3 multiply_reduce_fusion.2
  376.2 1.5 fusion.84
  377.7 1.5 fusion.83
  379.9 0.8 copy_dynamic-update-slice_fusion.2
  381.6 1.3 multiply_reduce_fusion.2
  383.5 1.5 fusion.84
  385.0 1.5 fusion.83
  387.2 0.7 copy_dynamic-update-slice_fusion.2
  388.8 1.3 multiply_reduce_fusion.2
  390.8 1.5 fusion.84
  392.3 1.5 fusion.83
  394.5 0.8 copy_dynamic-update-slice_fusion.2
  396.1 1.3 multiply_reduce_fusion.2
  398.1 1.5 fusion.84
  399.6 1.5 fusion.83
  401.8 0.8 copy_dynamic-update-slice_fusion.2
  403.4 1.3 multiply_reduce_fusion.2
  405.4 1.5 fusion.84
  406.9 1.5 fusion.83
  409.1 0.8 copy_dynamic-update-slice_fusion.2
  410.7 1.3 multiply_reduce_fusion.2
  412.6 1.5 fusion.84
  414.2 1.5 fusion.83
  416.3 0.8 copy_dynamic-update-slice_fusion.2
  417.1 2.3 reshape.298
  419.4 3.7 all-to-all-start.2
  423.0 18.2 %all-to-all-done.2 = bf16[16,64,512]{2,1,0:T(8,128)(2,1)S(1)} async-done(((bf16[16,64,512]{2,1,0:T(8,128)(2,1)}), bf16[16,64,512]{2,1,0:T(8,128)(2,1)S(1)}, u32[]{:S(2)}, u32[]{:S(2)}) %all-to-all-start.2) | async-done | bytes 1048608 | tf_op jit(solution)/shard_map/all_to_all | solution.py:151
  441.3 2.6 gather_fusion
  (145 shorter events, 19.8 us)
Async XLA Ops:
  6.5 302.2 %copy-start = (bf16[64,128,1,128]{3,1,2,0:T(8,128)(2,1)S(1)}, bf16[64,128,1,128]{3,1,2,0:T(8,128)(2,1)}, u32[]{:S(2)}) copy-start(bf16[64,128,1,128]{3,1,2,0:T(8,128)(2,1)} %param.19) | copy-start | bytes 6291460
  14.1 7.3 %copy-start.6 = (bf16[1024]{0:T(1024)(128)(2,1)S(1)}, bf16[1024]{0:T(1024)(128)(2,1)}, u32[]{:S(2)}) copy-start(bf16[1024]{0:T(1024)(128)(2,1)} %param.14) | copy-start | bytes 6148
  14.1 7.3 %copy-start.3 = (bf16[512,1024]{1,0:T(8,128)(2,1)S(1)}, bf16[512,1024]{1,0:T(8,128)(2,1)}, u32[]{:S(2)}) copy-start(bf16[512,1024]{1,0:T(8,128)(2,1)} %param.13) | copy-start | bytes 3145732
  14.1 194.2 %all-to-all-start = ((bf16[16,64,8,768]{3,1,2,0:T(8,128)(2,1)}), bf16[16,64,8,768]{3,1,2,0:T(8,128)(2,1)}, u32[]{:S(2)}, u32[]{:S(2)}) async-start(bf16[16,64,8,768]{3,1,2,0:T(8,128)(2,1)} %stack.2), calls=%async_computation | async-start | bytes 25165824 | tf_op jit(solution)/shard_map/all_to_all | solution.py:79
  21.3 272.5 %reduce-scatter.2.cloned.1.call-start = ((), (), s32[]{:S(2)}) async-start(), calls=%async_computation.4 | async-start | bytes 14155776 | tf_op jit(solution)/shard_map/reduce_scatter | solution.py:83
  224.2 0.7 copy-start.5
  301.4 7.3 %copy-start.7 = (s32[1,32]{1,0:T(1,128)S(1)}, s32[1,32]{1,0:T(1,128)}, u32[]{:S(2)}) copy-start(s32[1,32]{1,0:T(1,128)} %param.21) | copy-start | bytes 388
  301.4 40.7 %all-to-all-start.1 = ((bf16[16,80,768]{2,1,0:T(8,128)(2,1)}), bf16[16,80,768]{2,1,0:T(8,128)(2,1)}, u32[]{:S(2)}, u32[]{:S(2)}) async-start(bf16[16,80,768]{2,1,0:T(8,128)(2,1)} %pad_maximum_fusion), calls=%async_computation.2 | async-start | bytes 3932160 | tf_op jit(solution)/shard_map/all_to_all | solution.py:101
  351.6 1.3 copy-start.2
  363.2 1.5 copy-start.4
  370.4 1.5 copy-start.4
  377.7 1.5 copy-start.4
  385.0 1.5 copy-start.4
  392.3 1.5 copy-start.4
  399.6 1.5 copy-start.4
  406.9 1.5 copy-start.4
  414.2 1.5 copy-start.4
  419.4 21.9 %all-to-all-start.2 = ((bf16[16,64,512]{2,1,0:T(8,128)(2,1)}), bf16[16,64,512]{2,1,0:T(8,128)(2,1)S(1)}, u32[]{:S(2)}, u32[]{:S(2)}) async-start(bf16[16,64,512]{2,1,0:T(8,128)(2,1)} %reshape.298), calls=%async_computation.3 | async-start | bytes 2097152 | tf_op jit(solution)/shard_map/all_to_all | solution.py:151
  441.3 2.6 copy-start.1
Sparse Core Ops, SparseCore 0:
  224.4 69.3 reduce-scatter.1
